TPU v7x, 32 devices: a whole 2x2x4 slice. The times are simulated.
32 devices in a mesh: tm: 8 (over y, x, core), space: 4 (over z).
Axes of the slice: x: 2, y: 2, z: 4, core: 2. Of those that a mesh axis runs over, the one named last changes fastest.
Arguments:
- queries: bfloat16 [8, 4, 128, 1024], P('tm', 'space'), may hold values from -30 to 30
- key_vectors: bfloat16 [8, 4, 128, 1024], P('tm', 'space'), may hold values from -30 to 30
- value_vectors: bfloat16 [8, 4, 128, 1024], P('tm', 'space'), may hold values from -6 to 6
- key_blocks: int32 [8, 4, 2, 32], P('tm', 'space'), may hold values from 0 to 63, as said below
- block_count: int32 [8, 4, 2], P('tm', 'space'), may hold values from 1 to 32, as said below
Outputs:
- attention_out: bfloat16 [8, 4, 128, 1024], P('tm', 'space')
Inputs may be any that keep to these rules, and one draw needn't show every extreme that they name: `key_blocks`: A row's entries are distinct ids of blocks in the query block's own band or an adjacent one, of any frame group; its first entry is the query block itself. Only the first block_count entries of a list are used; on some devices a list uses all 32.
All inputs are finite; a program needn't handle non-finite values.
Results may differ from a plain program's by a relative error of at most 0.0044.
Values may be sent and summed in bfloat16 or wider, within the bound.
No kernel may reach another device: no remote copies, remote signals or barrier semaphores. Data moves between devices by JAX's collectives and lax.ppermute only.
A program may use at most 128 MiB of HBM per device.

v0:
```python
import jax
import jax.numpy as jnp
from jax import lax
from jax.sharding import PartitionSpec as P

HEADS = 8
HDIM = 128
BLOCK = 64
PICKS = 32


def with_halo(cells, sides, width):
    for axis, dim in sides:
        count = lax.axis_size(axis)
        ends = count - 1
        head = lax.slice_in_dim(cells, 0, width, axis=dim)
        tail = lax.slice_in_dim(cells, cells.shape[dim] - width, cells.shape[dim], axis=dim)
        cells = jnp.concatenate(
            [
                lax.ppermute(tail, axis, [(i, (i + 1) % count) for i in range(ends)]),
                cells,
                lax.ppermute(head, axis, [((i + 1) % count, i) for i in range(ends)]),
            ],
            axis=dim,
        )
    return cells


def on_device(queries, key_vectors, value_vectors, key_blocks, block_count):
    tokens_here = queries.shape[2]
    feature_width = queries.shape[3]
    blocks_here = tokens_here // BLOCK
    stacked = jnp.stack([key_vectors, value_vectors])
    banded = with_halo(stacked, (("space", 2),), 1)
    gathered = lax.all_gather(banded, "tm", axis=1, tiled=True)
    groups = gathered.shape[1]
    ordered = gathered.reshape(2, groups, 3, blocks_here, BLOCK, feature_width)
    tile_set = ordered.reshape(2, groups * 3 * blocks_here, BLOCK, feature_width)
    band_count = lax.axis_size("space")
    own_band = lax.axis_index("space")
    listed = key_blocks.reshape(blocks_here, PICKS)
    within = listed % blocks_here
    band_of = listed // blocks_here % band_count
    group_of = listed // (blocks_here * band_count)
    slots = (group_of * 3 + band_of - own_band + 1) * blocks_here + within
    chosen = tile_set[:, slots.reshape(-1)]
    keyset = chosen[0].reshape(blocks_here, PICKS * BLOCK, HEADS, HDIM)
    valset = chosen[1].reshape(blocks_here, PICKS * BLOCK, HEADS, HDIM)
    query_rows = queries.reshape(blocks_here, BLOCK, HEADS, HDIM)
    scores = jnp.einsum(
        "bqhd,bkhd->bhqk", query_rows, keyset, preferred_element_type=jnp.float32
    ) * HDIM ** (-0.5)
    usable = (jnp.arange(PICKS * BLOCK) // BLOCK)[None, :] < block_count.reshape(blocks_here, 1)
    scores = jnp.where(usable[:, None, None, :], scores, -1e30)
    peaks = jnp.max(scores, axis=-1, keepdims=True)
    weights = jnp.exp(scores - peaks)
    totals = jnp.sum(weights, axis=-1)
    rounded = weights.astype(jnp.bfloat16)
    blended = jnp.einsum("bhqk,bkhd->bqhd", rounded, valset, preferred_element_type=jnp.float32)
    result = blended / jnp.transpose(totals, (0, 2, 1))[:, :, :, None]
    return result.reshape(queries.shape).astype(jnp.bfloat16)


def solution(mesh):
    in_specs = (
        P("tm", "space", None, None),
        P("tm", "space", None, None),
        P("tm", "space", None, None),
        P("tm", "space", None, None),
        P("tm", "space", None),
    )
    out_specs = P("tm", "space", None, None)
    return jax.shard_map(
        on_device, mesh=mesh, in_specs=in_specs, out_specs=out_specs, check_vma=False
    )
```

profile of v0, /device:TPU:0, one launch (start us, length us, event | category | flops | bytes accessed | tf_op | source)
XLA Modules:
  0.0 168.3 jit_solution(12035285831225546549)
XLA Ops:
  6.5 0.0 all-gather.2.cloned.1.call-start
  6.5 1.1 pad_maximum_fusion.1
  7.6 5.0 %collective-permute-start = (bf16[2,1,1,128,1024]{4,3,2,1,0:T(8,128)(2,1)S(1)}, bf16[2,1,1,128,1024]{4,3,2,1,0:T(8,128)(2,1)S(1)}, u32[]{:S(2)}, u32[]{:S(2)}) collective-permute-start(bf16[2,1,1,128,1024]{4,3,2,1,0:T(8,128)(2,1)S(1)} %pad_maximum_fusion.1), channel_id=1, source_target_pairs={{0,1},{1,2},{2,3},{4,5},{5,6},{6,7},{8,9},{9,10},{10,11},{12,13},{... | collective-permute-start | bytes 1572872 | tf_op jit(solution)/shard_map/ppermute | solution.py:20
  12.6 1.3 collective-permute-start.1
  13.9 9.8 %collective-permute-done = bf16[2,1,1,128,1024]{4,3,2,1,0:T(8,128)(2,1)S(1)} collective-permute-done((bf16[2,1,1,128,1024]{4,3,2,1,0:T(8,128)(2,1)S(1)}, bf16[2,1,1,128,1024]{4,3,2,1,0:T(8,128)(2,1)S(1)}, u32[]{:S(2)}, u32[]{:S(2)}) %collective-permute-start) | collective-permute-done | bytes 524320 | tf_op jit(solution)/shard_map/ppermute | solution.py:20
  23.7 4.1 %collective-permute-done.1 = bf16[2,1,1,128,1024]{4,3,2,1,0:T(8,128)(2,1)S(1)} collective-permute-done((bf16[2,1,1,128,1024]{4,3,2,1,0:T(8,128)(2,1)S(1)}, bf16[2,1,1,128,1024]{4,3,2,1,0:T(8,128)(2,1)S(1)}, u32[]{:S(2)}, u32[]{:S(2)}) %collective-permute-start.1) | collective-permute-done | bytes 524320 | tf_op jit(solution)/shard_map/ppermute | solution.py:22
  27.9 2.4 %pad_maximum_fusion = bf16[2,1,3,128,1024]{4,3,2,1,0:T(8,128)(2,1)} fusion(bf16[2,1,1,128,1024]{4,3,2,1,0:T(8,128)(2,1)S(1)} %collective-permute-done.1, bf16[1,1,1,128,1024]{4,3,2,1,0:T(8,128)(2,1)} %bitcast.56, bf16[1,1,1,128,1024]{4,3,2,1,0:T(8,128)(2,1)} %bitcast.58, bf16[2,1,1,128,1024]{4,3,2,1,0:T(8,128)(2,1)S(1)} %collective-permute-done), kind=kLoop, calls=%fused_computation.15 | loop fusion | flops 2359296 | bytes 3145728 | tf_op jit(solution)/shard_map/concatenate | solution.py:18
  30.2 0.0 all-gather.2.cloned.1.call-update
  30.3 0.8 reshape.249
  31.0 1.0 copy.16
  32.1 0.7 broadcast_compare_fusion
  32.8 69.9 %all-gather.2.cloned.1.call-done = bf16[2,8,3,128,1024]{4,3,2,1,0:T(8,128)(2,1)} async-done(((bf16[2,1,3,128,1024]{4,3,2,1,0:T(8,128)(2,1)}), bf16[2,8,3,128,1024]{4,3,2,1,0:T(8,128)(2,1)}) %all-gather.2.cloned.1.call-update) | async-done | bytes 12582928 | tf_op jit(solution)/shard_map/all_gather | solution.py:35
  102.7 12.2 %gather_fusion = bf16[64,2,64,1024]{3,2,1,0:T(8,128)(2,1)} fusion(bf16[2,48,64,1024]{3,2,1,0:T(8,128)(2,1)} %bitcast.52, s32[1024]{0:T(1024)S(1)} %pad_clamp_fusion), kind=kCustom, calls=%fused_computation | custom fusion | bytes 33554688 | tf_op jit(solution)/shard_map/gather | solution.py:46
  114.9 12.1 %fusion.37 = (bf16[1,64,64,1024]{3,2,0,1:T(8,128)(2,1)}, bf16[1,64,64,1024]{3,2,0,1:T(8,128)(2,1)}) fusion(bf16[2,64,64,1024]{3,2,0,1:T(8,128)(2,1)} %bitcast.49), kind=kLoop, calls=%fused_computation.48 | loop fusion | bytes 33554432 | tf_op jit(solution)/shard_map/slice | solution.py:47
  127.1 8.8 %copy.15 = bf16[512,8,8,128]{3,2,1,0:T(8,128)(2,1)} copy(bf16[512,8,8,128]{3,1,2,0:T(8,128)(2,1)} %bitcast.51) | data formatting | bytes 16777216
  135.8 8.8 %copy.17 = bf16[512,8,8,128]{3,2,1,0:T(8,128)(2,1)} copy(bf16[512,8,8,128]{3,1,2,0:T(8,128)(2,1)} %bitcast.50) | data formatting | bytes 16777216
  144.6 7.2 %bitcast_reduce_fusion = (f32[2,8,64]{2,1,0:T(8,128)S(1)}, f32[2,8,2048,64]{2,3,1,0:T(8,128)S(1)}) fusion(pred[2,2048]{1,0:T(4,128)(4,1)S(1)} %broadcast_compare_fusion, bf16[2,64,8,128]{3,2,1,0:T(8,128)(2,1)S(1)} %bitcast.60, bf16[2,2048,8,128]{3,2,1,0:T(8,128)(2,1)} %bitcast.54), kind=kOutput, calls=%fused_computation.2 | convolution fusion | flops 543161344 | bytes 17047552 | tf_op jit(solution)/shard_map/bqhd,bkhd->bhqk/dot_general | solution.py:50
  151.8 2.1 %fusion.5 = f32[2,8,64]{2,1,0:T(8,128)S(1)} fusion(f32[2,8,2048,64]{2,3,1,0:T(8,128)S(1)} %get-tuple-element.8, f32[2,8,64]{2,1,0:T(8,128)S(1)} %get-tuple-element.7, pred[2,2048]{1,0:T(4,128)(4,1)S(1)} %broadcast_compare_fusion), kind=kLoop, calls=%fused_computation.9 | loop fusion | flops 8387584 | bytes 8400896 | tf_op jit(solution)/shard_map/reduce_sum | solution.py:57
  153.8 6.6 %fusion.22 = bf16[2,64,8,128]{3,1,2,0:T(8,128)(2,1)S(1)} fusion(bf16[2,2048,8,128]{3,2,1,0:T(8,128)(2,1)} %bitcast.53, f32[2,8,2048,64]{2,3,1,0:T(8,128)S(1)} %get-tuple-element.8, f32[2,8,64]{2,1,0:T(8,128)S(1)} %get-tuple-element.7, pred[2,2048]{1,0:T(4,128)(4,1)S(1)} %broadcast_compare_fusion, f32[2,64,8]{1,2,0:T(8,128)S(1)} %bitcast.61), kind=kOutput, calls=%fused_computation.18 | convolution fusion | flops 545521664 | bytes 17051648 | tf_op jit(solution)/shard_map/bhqk,bkhd->bqhd/dot_general | solution.py:59
  160.4 0.2 copy.14
  160.6 0.8 convert_element_type.19
  (3 shorter events, 0.0 us)
Async XLA Ops:
  6.5 96.2 %all-gather.2.cloned.1.call-start = ((), (), s32[]{:S(2)}) async-start(), calls=%async_computation | async-start | bytes 14155776 | tf_op jit(solution)/shard_map/all_gather | solution.py:35
  7.6 16.1 %collective-permute-start = (bf16[2,1,1,128,1024]{4,3,2,1,0:T(8,128)(2,1)S(1)}, bf16[2,1,1,128,1024]{4,3,2,1,0:T(8,128)(2,1)S(1)}, u32[]{:S(2)}, u32[]{:S(2)}) collective-permute-start(bf16[2,1,1,128,1024]{4,3,2,1,0:T(8,128)(2,1)S(1)} %pad_maximum_fusion.1), channel_id=1, source_target_pairs={{0,1},{1,2},{2,3},{4,5},{5,6},{6,7},{8,9},{9,10},{10,11},{12,13},{... | collective-permute-start | bytes 1572872 | tf_op jit(solution)/shard_map/ppermute | solution.py:20
  12.6 15.3 %collective-permute-start.1 = (bf16[2,1,1,128,1024]{4,3,2,1,0:T(8,128)(2,1)S(1)}, bf16[2,1,1,128,1024]{4,3,2,1,0:T(8,128)(2,1)S(1)}, u32[]{:S(2)}, u32[]{:S(2)}) collective-permute-start(bf16[2,1,1,128,1024]{4,3,2,1,0:T(8,128)(2,1)S(1)} %pad_maximum_fusion.1), channel_id=1, source_target_pairs={{1,0},{2,1},{3,2},{5,4},{6,5},{7,6},{9,8},{10,9},{11,10},{13,12},{... | collective-permute-start | bytes 1572872 | tf_op jit(solution)/shard_map/ppermute | solution.py:22
Sparse Core Ops, SparseCore 0:
  30.4 72.3 all-gather.1
where the time goes:
time: 169 us; the launch traced here: 168 us
  waiting for transfers between devices  83.9 us (50%)
  local copies, waits for them, and re-layouts  44.6 us (26%)
  matrix products  13.8 us (8%)
  between operations  13.5 us (8%)
  other arithmetic  6.27 us (4%)
  starting transfers between devices  6.25 us (4%)
    all_gather x1, waiting for transfers between devices, on_device(): gathered = lax.all_gather(banded, 'tm', axis=1, tiled=True)  69.9 us
    unnamed x3, local copies, waits for them, and re-layouts  18.5 us
    gather x1, local copies, waits for them, and re-layouts, on_device(): chosen = tile_set[:, slots.reshape(-1)]  12.2 us
    slice x1, local copies, waits for them, and re-layouts, on_device(): keyset = chosen[0].reshape(blocks_here, PICKS * BLOCK, HEADS, HDIM)  12.1 us
    ppermute x1, waiting for transfers between devices, with_halo(): lax.ppermute(tail, axis, [(i, (i + 1) % count) for i in range(ends)])  9.83 us
    dot_general x1, matrix products, on_device(): jnp.einsum('bqhd,bkhd->bhqk', query_rows, keyset, preferred_element_type=...  7.19 us
    dot_general x1, matrix products, on_device(): jnp.einsum('bhqk,bkhd->bqhd', rounded, valset, preferred_element_type=jnp...  6.57 us
    ppermute x1, starting transfers between devices, with_halo(): lax.ppermute(tail, axis, [(i, (i + 1) % count) for i in range(ends)])  4.96 us
  transfers between devices with their start and end apart: 3, of which 3 were waited for; matrix products, arithmetic and copies ran while one was open for 2% of the time, Pallas kernels for 0%

commit v1 on v0

--- a/solution.py
+++ b/solution.py
@@ -7,6 +7,18 @@
 HDIM = 128
 BLOCK = 64
 PICKS = 32
+
+
+def doubled_up(value, axis, dim):
+    ways, here, step = (lax.axis_size(axis), lax.axis_index(axis), value.shape[dim])
+    line, have = (value, 1)
+    while have < ways:
+        line = jnp.concatenate(
+            [line, lax.ppermute(line, axis, [(d, (d - have) % ways) for d in range(ways)])],
+            axis=dim,
+        )
+        have = 2 * have
+    return jnp.roll(line, here * step, axis=dim)
 
 
 def with_halo(cells, sides, width):
@@ -32,7 +44,7 @@
     blocks_here = tokens_here // BLOCK
     stacked = jnp.stack([key_vectors, value_vectors])
     banded = with_halo(stacked, (("space", 2),), 1)
-    gathered = lax.all_gather(banded, "tm", axis=1, tiled=True)
+    gathered = doubled_up(banded, "tm", 1)
     groups = gathered.shape[1]
     ordered = gathered.reshape(2, groups, 3, blocks_here, BLOCK, feature_width)
     tile_set = ordered.reshape(2, groups * 3 * blocks_here, BLOCK, feature_width)

time: 169 us -> 345 us (2.04)
  waiting for transfers between devices: 83.9 us -> 233 us
  local copies, waits for them, and re-layouts: 44.6 us -> 76.1 us
  between operations: 13.5 us -> 0.12 us
  other arithmetic: 6.27 us -> 12.8 us
    ppermute x0 -> x3, waiting for transfers between devices: none -> 219 us  [doubled_up(): lax.ppermute(line, axis, [(d, (d - have) % ways) for d in range(ways)])]
    all_gather x1 -> x0, waiting for transfers between devices: 69.9 us -> none  [on_device(): gathered = lax.all_gather(banded, 'tm', axis=1, tiled=True)]
    unnamed x3 -> x36, local copies, waits for them, and re-layouts: 18.5 us -> 33.5 us
    dynamic_slice x0 -> x1, local copies, waits for them, and re-layouts: none -> 10.6 us  [doubled_up(): return jnp.roll(line, here * step, axis=dim)]
    concatenate x0 -> x1, local copies, waits for them, and re-layouts: none -> 6.54 us  [doubled_up(): return jnp.roll(line, here * step, axis=dim)]
    concatenate x0 -> x2, other arithmetic: none -> 5.47 us  [doubled_up(): jnp.concatenate([line, lax.ppermute(line, axis, [(d, (d - have) % ways) f...]
  transfers between devices with their start and end apart: 3 -> 5, of which waited for: 3 -> 5; matrix products, arithmetic and copies ran while one was open for 2% -> 2% of each run, Pallas kernels for 0% -> 0%
where the time goes in v1:
time: 345 us; the launch traced here: 344 us
  waiting for transfers between devices  233 us (68%)
  local copies, waits for them, and re-layouts  76.1 us (22%)
  matrix products  13.8 us (4%)
  other arithmetic  12.8 us (4%)
  starting transfers between devices  8.98 us (3%)
    ppermute x3, waiting for transfers between devices, doubled_up(): lax.ppermute(line, axis, [(d, (d - have) % ways) for d in range(ways)])  219 us
    unnamed x36, local copies, waits for them, and re-layouts  33.5 us
    gather x1, local copies, waits for them, and re-layouts, on_device(): chosen = tile_set[:, slots.reshape(-1)]  12.2 us
    slice x1, local copies, waits for them, and re-layouts, on_device(): keyset = chosen[0].reshape(blocks_here, PICKS * BLOCK, HEADS, HDIM)  12.2 us
    dynamic_slice x1, local copies, waits for them, and re-layouts, doubled_up(): return jnp.roll(line, here * step, axis=dim)  10.6 us
    ppermute x1, waiting for transfers between devices, with_halo(): lax.ppermute(tail, axis, [(i, (i + 1) % count) for i in range(ends)])  9.83 us
    dot_general x1, matrix products, on_device(): jnp.einsum('bqhd,bkhd->bhqk', query_rows, keyset, preferred_element_type=...  7.19 us
  transfers between devices with their start and end apart: 5, of which 5 were waited for; matrix products, arithmetic and copies ran while one was open for 2% of the time, Pallas kernels for 0%

profile of v1, /device:TPU:0, one launch (start us, length us, event | category | flops | bytes accessed | tf_op | source)
XLA Modules:
  0.0 344.4 jit_solution(17912533632691151019)
XLA Ops:
  0.0 0.0 copy-start.9
  0.0 0.0 copy-start.8
  0.0 1.1 pad_maximum_fusion.6
  1.1 0.0 copy-start.6
  1.2 5.0 %collective-permute-start = (bf16[2,1,1,128,1024]{4,3,2,1,0:T(8,128)(2,1)S(1)}, bf16[2,1,1,128,1024]{4,3,2,1,0:T(8,128)(2,1)S(1)}, u32[]{:S(2)}, u32[]{:S(2)}) collective-permute-start(bf16[2,1,1,128,1024]{4,3,2,1,0:T(8,128)(2,1)S(1)} %pad_maximum_fusion.6), channel_id=1, source_target_pairs={{0,1},{1,2},{2,3},{4,5},{5,6},{6,7},{8,9},{9,10},{10,11},{12,13},{... | collective-permute-start | bytes 1572872 | tf_op jit(solution)/shard_map/ppermute | solution.py:32
  6.1 1.3 collective-permute-start.1
  7.4 9.8 %collective-permute-done = bf16[2,1,1,128,1024]{4,3,2,1,0:T(8,128)(2,1)S(1)} collective-permute-done((bf16[2,1,1,128,1024]{4,3,2,1,0:T(8,128)(2,1)S(1)}, bf16[2,1,1,128,1024]{4,3,2,1,0:T(8,128)(2,1)S(1)}, u32[]{:S(2)}, u32[]{:S(2)}) %collective-permute-start) | collective-permute-done | bytes 524320 | tf_op jit(solution)/shard_map/ppermute | solution.py:32
  17.3 0.0 copy-start.2
  17.3 4.1 %collective-permute-done.1 = bf16[2,1,1,128,1024]{4,3,2,1,0:T(8,128)(2,1)S(1)} collective-permute-done((bf16[2,1,1,128,1024]{4,3,2,1,0:T(8,128)(2,1)S(1)}, bf16[2,1,1,128,1024]{4,3,2,1,0:T(8,128)(2,1)S(1)}, u32[]{:S(2)}, u32[]{:S(2)}) %collective-permute-start.1) | collective-permute-done | bytes 524320 | tf_op jit(solution)/shard_map/ppermute | solution.py:34
  21.4 0.0 copy-start.4
  21.4 2.7 pad_maximum_fusion.2
  24.1 0.0 copy-start.13
  24.1 0.0 copy-start.10
  24.1 0.0 copy-start.12
  24.1 0.7 collective-permute-start.2
  24.8 17.9 %collective-permute-done.2 = bf16[2,1,3,128,1024]{4,3,2,1,0:T(8,128)(2,1)S(1)} collective-permute-done((bf16[2,1,3,128,1024]{4,3,2,1,0:T(8,128)(2,1)S(1)}, bf16[2,1,3,128,1024]{4,3,2,1,0:T(8,128)(2,1)S(1)}, u32[]{:S(2)}, u32[]{:S(2)}) %collective-permute-start.2) | collective-permute-done | bytes 1572896 | tf_op jit(solution)/shard_map/ppermute | solution.py:17
  42.7 0.0 copy-start
  42.8 1.8 pad_maximum_fusion.1
  44.6 1.8 collective-permute-start.3
  46.4 69.1 %collective-permute-done.3 = bf16[2,2,3,128,1024]{4,3,2,1,0:T(8,128)(2,1)S(1)} collective-permute-done((bf16[2,2,3,128,1024]{4,3,2,1,0:T(8,128)(2,1)S(1)}, bf16[2,2,3,128,1024]{4,3,2,1,0:T(8,128)(2,1)S(1)}, u32[]{:S(2)}, u32[]{:S(2)}) %collective-permute-start.3) | collective-permute-done | bytes 3145760 | tf_op jit(solution)/shard_map/ppermute | solution.py:17
  115.5 0.0 copy-done.9
  115.5 0.0 copy-done.8
  115.5 3.6 %pad_maximum_fusion = bf16[2,4,3,128,1024]{4,3,2,1,0:T(8,128)(2,1)} fusion(bf16[2,2,3,128,1024]{4,3,2,1,0:T(8,128)(2,1)S(1)} %collective-permute-done.3, bf16[2,1,3,128,1024]{4,3,2,1,0:T(8,128)(2,1)S(1)} %collective-permute-done.2, bf16[2,1,1,128,1024]{4,3,2,1,0:T(8,128)(2,1)S(1)} %collective-permute-done.1, bf16[1,1,1,128,1024]{4,3,2,1,0:T(8,128)(2,1)S(1)} %bitcast.58, ...), kind=kLoop, calls=%fused_computation.11 | loop fusion | flops 15728640 | bytes 12582912 | tf_op jit(solution)/shard_map/concatenate | solution.py:16
  119.2 0.0 copy-done.6
  119.2 0.0 copy-done.2
  119.2 0.0 copy-done.4
  119.2 0.0 copy-done
  119.2 0.2 collective-permute-start.4
  119.4 0.0 copy-done.13
  119.4 0.1 reshape.249
  119.5 0.0 copy-done.10
  119.5 0.8 copy.16
  120.3 0.0 copy-done.12
  120.3 0.1 broadcast_compare_fusion
  120.4 2.8 constant_dynamic-update-slice_fusion.5
  123.2 0.0 copy-start.3
  123.2 0.0 copy-start.5
  123.2 0.0 copy-start.7
  123.2 2.2 constant_dynamic-update-slice_fusion.4
  125.4 0.0 copy-start.1
  125.4 131.7 %collective-permute-done.4 = bf16[2,4,3,128,1024]{4,3,2,1,0:T(8,128)(2,1)} collective-permute-done((bf16[2,4,3,128,1024]{4,3,2,1,0:T(8,128)(2,1)}, bf16[2,4,3,128,1024]{4,3,2,1,0:T(8,128)(2,1)}, u32[]{:S(2)}, u32[]{:S(2)}) %collective-permute-start.4) | collective-permute-done | bytes 6291488 | tf_op jit(solution)/shard_map/ppermute | solution.py:17
  257.1 6.4 %constant_dynamic-update-slice_fusion.3 = bf16[2,16,3,128,1024]{4,3,2,1,0:T(8,128)(2,1)} fusion(bf16[2,16,3,128,1024]{4,3,2,1,0:T(8,128)(2,1)} %constant_dynamic-update-slice_fusion.4, bf16[2,4,3,128,1024]{4,3,2,1,0:T(8,128)(2,1)} %collective-permute-done.4), kind=kLoop, calls=%fused_computation.31 | loop fusion | bytes 12582912
  263.5 0.0 copy-done.3
  263.5 0.0 copy-done.5
  263.5 0.0 copy-done.7
  263.5 1.3 fusion.27
  264.8 0.0 copy-done.1
  264.8 1.3 constant_dynamic-update-slice_fusion.2
  266.1 2.4 constant_dynamic-update-slice_fusion.1
  268.4 6.5 %constant_dynamic-update-slice_fusion = bf16[2,16,3,128,1024]{4,3,2,1,0:T(8,128)(2,1)} fusion(bf16[2,16,3,128,1024]{4,3,2,1,0:T(8,128)(2,1)} %constant_dynamic-update-slice_fusion.1, bf16[2,4,3,128,1024]{4,3,2,1,0:T(8,128)(2,1)} %collective-permute-done.4), kind=kLoop, calls=%fused_computation.28 | loop fusion | bytes 12582912 | tf_op jit(solution)/shard_map/jit(_roll_dynamic)/concatenate | solution.py:21
  275.0 10.6 %constant_dynamic-slice_fusion = bf16[2,8,3,128,1024]{4,3,2,1,0:T(8,128)(2,1)} fusion(bf16[2,16,3,128,1024]{4,3,2,1,0:T(8,128)(2,1)} %constant_dynamic-update-slice_fusion, s32[]{:T(128)S(6)} %select_n.90), kind=kLoop, calls=%fused_computation.59 | loop fusion | bytes 25165828 | tf_op jit(solution)/shard_map/jit(_roll_dynamic)/dynamic_slice | solution.py:21
  285.6 12.2 %gather_fusion = bf16[64,2,64,1024]{3,2,1,0:T(8,128)(2,1)} fusion(bf16[2,48,64,1024]{3,2,1,0:T(8,128)(2,1)} %bitcast.49, s32[1024]{0:T(1024)S(1)} %pad_clamp_fusion), kind=kCustom, calls=%fused_computation | custom fusion | bytes 33554688 | tf_op jit(solution)/shard_map/gather | solution.py:58
  297.8 12.2 %fusion.39 = (bf16[1,64,64,1024]{3,2,0,1:T(8,128)(2,1)}, bf16[1,64,64,1024]{3,2,0,1:T(8,128)(2,1)}) fusion(bf16[2,64,64,1024]{3,2,0,1:T(8,128)(2,1)} %bitcast.50), kind=kLoop, calls=%fused_computation.62 | loop fusion | bytes 33554432 | tf_op jit(solution)/shard_map/slice | solution.py:59
  310.0 8.8 %copy.15 = bf16[512,8,8,128]{3,2,1,0:T(8,128)(2,1)} copy(bf16[512,8,8,128]{3,1,2,0:T(8,128)(2,1)} %bitcast.52) | data formatting | bytes 16777216
  318.7 0.0 copy-start.11
  318.7 8.8 %copy.17 = bf16[512,8,8,128]{3,2,1,0:T(8,128)(2,1)} copy(bf16[512,8,8,128]{3,1,2,0:T(8,128)(2,1)} %bitcast.51) | data formatting | bytes 16777216
  327.6 0.0 copy-done.11
  327.6 7.2 %bitcast_reduce_fusion = (f32[2,8,64]{2,1,0:T(8,128)S(1)}, f32[2,8,2048,64]{2,3,1,0:T(8,128)S(1)}) fusion(pred[2,2048]{1,0:T(4,128)(4,1)S(1)} %broadcast_compare_fusion, bf16[2,64,8,128]{3,2,1,0:T(8,128)(2,1)S(1)} %bitcast.64, bf16[2,2048,8,128]{3,2,1,0:T(8,128)(2,1)} %bitcast.54), kind=kOutput, calls=%fused_computation.2 | convolution fusion | flops 543161344 | bytes 17047552 | tf_op jit(solution)/shard_map/bqhd,bkhd->bhqk/dot_general | solution.py:62
  334.8 2.1 fusion.5
  336.9 6.6 %fusion.22 = bf16[2,64,8,128]{3,1,2,0:T(8,128)(2,1)S(1)} fusion(bf16[2,2048,8,128]{3,2,1,0:T(8,128)(2,1)} %bitcast.53, f32[2,8,2048,64]{2,3,1,0:T(8,128)S(1)} %get-tuple-element.10, f32[2,8,64]{2,1,0:T(8,128)S(1)} %get-tuple-element.9, pred[2,2048]{1,0:T(4,128)(4,1)S(1)} %broadcast_compare_fusion, f32[2,64,8]{1,2,0:T(8,128)S(1)} %bitcast.65), kind=kOutput, calls=%fused_computation.23 | convolution fusion | flops 545521664 | bytes 17051648 | tf_op jit(solution)/shard_map/bhqk,bkhd->bqhd/dot_general | solution.py:71
  343.4 0.2 copy.14
  343.6 0.8 convert_element_type.19
  (3 shorter events, 0.0 us)
Async XLA Ops:
  0.0 115.5 %copy-start.9 = (bf16[1,1,128,1024]{3,2,1,0:T(8,128)(2,1)S(1)}, bf16[1,1,128,1024]{3,2,1,0:T(8,128)(2,1)}, u32[]{:S(2)}) copy-start(bf16[1,1,128,1024]{3,2,1,0:T(8,128)(2,1)} %param.6) | copy-start | bytes 786436
  0.0 115.5 %copy-start.8 = (bf16[1,1,128,1024]{3,2,1,0:T(8,128)(2,1)S(1)}, bf16[1,1,128,1024]{3,2,1,0:T(8,128)(2,1)}, u32[]{:S(2)}) copy-start(bf16[1,1,128,1024]{3,2,1,0:T(8,128)(2,1)} %param.7) | copy-start | bytes 786436
  1.1 118.0 %copy-start.6 = (bf16[2,1,1,128,1024]{4,3,2,1,0:T(8,128)(2,1)}, bf16[2,1,1,128,1024]{4,3,2,1,0:T(8,128)(2,1)S(1)}, u32[]{:S(2)}) copy-start(bf16[2,1,1,128,1024]{4,3,2,1,0:T(8,128)(2,1)S(1)} %pad_maximum_fusion.6) | copy-start | bytes 1572868
  1.2 16.1 %collective-permute-start = (bf16[2,1,1,128,1024]{4,3,2,1,0:T(8,128)(2,1)S(1)}, bf16[2,1,1,128,1024]{4,3,2,1,0:T(8,128)(2,1)S(1)}, u32[]{:S(2)}, u32[]{:S(2)}) collective-permute-start(bf16[2,1,1,128,1024]{4,3,2,1,0:T(8,128)(2,1)S(1)} %pad_maximum_fusion.6), channel_id=1, source_target_pairs={{0,1},{1,2},{2,3},{4,5},{5,6},{6,7},{8,9},{9,10},{10,11},{12,13},{... | collective-permute-start | bytes 1572872 | tf_op jit(solution)/shard_map/ppermute | solution.py:32
  6.1 15.3 %collective-permute-start.1 = (bf16[2,1,1,128,1024]{4,3,2,1,0:T(8,128)(2,1)S(1)}, bf16[2,1,1,128,1024]{4,3,2,1,0:T(8,128)(2,1)S(1)}, u32[]{:S(2)}, u32[]{:S(2)}) collective-permute-start(bf16[2,1,1,128,1024]{4,3,2,1,0:T(8,128)(2,1)S(1)} %pad_maximum_fusion.6), channel_id=1, source_target_pairs={{1,0},{2,1},{3,2},{5,4},{6,5},{7,6},{9,8},{10,9},{11,10},{13,12},{... | collective-permute-start | bytes 1572872 | tf_op jit(solution)/shard_map/ppermute | solution.py:34
  17.3 101.9 %copy-start.2 = (bf16[2,1,1,128,1024]{4,3,2,1,0:T(8,128)(2,1)}, bf16[2,1,1,128,1024]{4,3,2,1,0:T(8,128)(2,1)S(1)}, u32[]{:S(2)}) copy-start(bf16[2,1,1,128,1024]{4,3,2,1,0:T(8,128)(2,1)S(1)} %collective-permute-done) | copy-start | bytes 1572868
  21.4 97.8 %copy-start.4 = (bf16[2,1,1,128,1024]{4,3,2,1,0:T(8,128)(2,1)}, bf16[2,1,1,128,1024]{4,3,2,1,0:T(8,128)(2,1)S(1)}, u32[]{:S(2)}) copy-start(bf16[2,1,1,128,1024]{4,3,2,1,0:T(8,128)(2,1)S(1)} %collective-permute-done.1) | copy-start | bytes 1572868
  24.1 95.3 %copy-start.13 = (s32[1,1,2,32]{3,2,1,0:T(2,128)S(1)}, s32[1,1,2,32]{3,2,1,0:T(2,128)}, u32[]{:S(2)}) copy-start(s32[1,1,2,32]{3,2,1,0:T(2,128)} %param.8) | copy-start | bytes 772
  24.1 95.4 %copy-start.10 = (bf16[1,1,128,1024]{3,2,1,0:T(8,128)(2,1)S(1)}, bf16[1,1,128,1024]{3,2,1,0:T(8,128)(2,1)}, u32[]{:S(2)}) copy-start(bf16[1,1,128,1024]{3,2,1,0:T(8,128)(2,1)} %param.5) | copy-start | bytes 786436
  24.1 96.2 %copy-start.12 = (s32[1,1,2]{2,1,0:T(1,128)S(1)}, s32[1,1,2]{2,1,0:T(1,128)}, u32[]{:S(2)}) copy-start(s32[1,1,2]{2,1,0:T(1,128)} %param.9) | copy-start | bytes 28
  24.1 18.6 %collective-permute-start.2 = (bf16[2,1,3,128,1024]{4,3,2,1,0:T(8,128)(2,1)S(1)}, bf16[2,1,3,128,1024]{4,3,2,1,0:T(8,128)(2,1)S(1)}, u32[]{:S(2)}, u32[]{:S(2)}) collective-permute-start(bf16[2,1,3,128,1024]{4,3,2,1,0:T(8,128)(2,1)S(1)} %get-tuple-element.7), channel_id=1, source_target_pairs={{0,28},{4,0},{8,4},{12,8},{16,12},{20,16},{24,20},{28,24},{1,29},{... | collective-permute-start | bytes 4718600 | tf_op jit(solution)/shard_map/ppermute | solution.py:17
  42.7 76.4 %copy-start = (bf16[2,1,3,128,1024]{4,3,2,1,0:T(8,128)(2,1)}, bf16[2,1,3,128,1024]{4,3,2,1,0:T(8,128)(2,1)S(1)}, u32[]{:S(2)}) copy-start(bf16[2,1,3,128,1024]{4,3,2,1,0:T(8,128)(2,1)S(1)} %collective-permute-done.2) | copy-start | bytes 4718596
  44.6 70.9 %collective-permute-start.3 = (bf16[2,2,3,128,1024]{4,3,2,1,0:T(8,128)(2,1)S(1)}, bf16[2,2,3,128,1024]{4,3,2,1,0:T(8,128)(2,1)S(1)}, u32[]{:S(2)}, u32[]{:S(2)}) collective-permute-start(bf16[2,2,3,128,1024]{4,3,2,1,0:T(8,128)(2,1)S(1)} %pad_maximum_fusion.1), channel_id=1, source_target_pairs={{0,24},{4,28},{8,0},{12,4},{16,8},{20,12},{24,16},{28,20},{1,25},{... | collective-permute-start | bytes 9437192 | tf_op jit(solution)/shard_map/ppermute | solution.py:17
  119.2 137.9 %collective-permute-start.4 = (bf16[2,4,3,128,1024]{4,3,2,1,0:T(8,128)(2,1)}, bf16[2,4,3,128,1024]{4,3,2,1,0:T(8,128)(2,1)}, u32[]{:S(2)}, u32[]{:S(2)}) collective-permute-start(bf16[2,4,3,128,1024]{4,3,2,1,0:T(8,128)(2,1)} %pad_maximum_fusion), channel_id=1, source_target_pairs={{0,16},{4,20},{8,24},{12,28},{16,0},{20,4},{24,8},{28,12},{1,17},{... | collective-permute-start | bytes 18874376 | tf_op jit(solution)/shard_map/ppermute | solution.py:17
  123.2 140.3 %copy-start.3 = (bf16[2,1,1,128,1024]{4,3,2,1,0:T(8,128)(2,1)S(1)}, bf16[2,1,1,128,1024]{4,3,2,1,0:T(8,128)(2,1)}, u32[]{:S(2)}) copy-start(bf16[2,1,1,128,1024]{4,3,2,1,0:T(8,128)(2,1)} %copy-done.2) | copy-start | bytes 1572868
  123.2 140.3 %copy-start.5 = (bf16[2,1,1,128,1024]{4,3,2,1,0:T(8,128)(2,1)S(1)}, bf16[2,1,1,128,1024]{4,3,2,1,0:T(8,128)(2,1)}, u32[]{:S(2)}) copy-start(bf16[2,1,1,128,1024]{4,3,2,1,0:T(8,128)(2,1)} %copy-done.4) | copy-start | bytes 1572868
  123.2 140.3 %copy-start.7 = (bf16[2,1,1,128,1024]{4,3,2,1,0:T(8,128)(2,1)S(1)}, bf16[2,1,1,128,1024]{4,3,2,1,0:T(8,128)(2,1)}, u32[]{:S(2)}) copy-start(bf16[2,1,1,128,1024]{4,3,2,1,0:T(8,128)(2,1)} %copy-done.6) | copy-start | bytes 1572868
  125.4 139.4 %copy-start.1 = (bf16[2,1,3,128,1024]{4,3,2,1,0:T(8,128)(2,1)S(1)}, bf16[2,1,3,128,1024]{4,3,2,1,0:T(8,128)(2,1)}, u32[]{:S(2)}) copy-start(bf16[2,1,3,128,1024]{4,3,2,1,0:T(8,128)(2,1)} %copy-done) | copy-start | bytes 4718596
  318.7 8.8 %copy-start.11 = (bf16[16,8,8,128]{3,2,1,0:T(8,128)(2,1)S(1)}, bf16[16,8,8,128]{3,2,1,0:T(8,128)(2,1)}, u32[]{:S(2)}) copy-start(bf16[16,8,8,128]{3,2,1,0:T(8,128)(2,1)} %copy.16) | copy-start | bytes 786436
